TPU v7x, 32 devices: a whole 2x2x4 slice. The times are simulated.
32 devices in a mesh: section: 2 (over x), fsdp: 4 (over z), dp: 4 (over y, core).
Axes of the slice: x: 2, y: 2, z: 4, core: 2. Of those that a mesh axis runs over, the one named last changes fastest.
Arguments:
- activations: bfloat16 [2, 4, 512, 3584], P('section', None, ('fsdp', 'dp')), may hold values from -6 to 6
- out_grad: bfloat16 [2, 4, 512, 14336], P('section', None, ('fsdp', 'dp')), may hold values from -6 to 6
- blocks: bfloat16 [2, 16, 128, 128], P('section', 'fsdp'), may hold values from -0.5 to 0.5
- pattern: int32 [2, 16, 2], P('section', 'fsdp'), may hold values from 0 to 111, as said below
- order: int32 [4], replicated, may hold values from 0 to 3, each once
Outputs:
- received: bfloat16 [2, 4, 512, 3584], P('section', None, ('fsdp', 'dp'))
- weight_grad: float32 [2, 16, 128, 128], P('section', 'fsdp')
Inputs may be any that keep to these rules, and one draw needn't show every extreme that they name: pattern[s, b, 0] < 28 and pattern[s, b, 1] < 112; no two blocks of one section share both indices; within a section the blocks stand in ascending order of (row, column). `order`: a permutation of the microbatches.
All inputs are finite; a program needn't handle non-finite values.
Results may differ from a plain program's by a relative error of at most 0.0049.
Values may be sent and summed in bfloat16 or wider, within the bound.
No kernel may reach another device: no remote copies, remote signals or barrier semaphores. Data moves between devices by JAX's collectives and lax.ppermute only.
A program may use at most 128 MiB of HBM per device.

v0:
```python
import math
import jax
import jax.numpy as jnp
from jax import lax
from jax.sharding import PartitionSpec as P


def passed_along(block, axis, distance):
    devices = range(lax.axis_size(axis))
    route = [(i - distance, i) for i in devices if i - distance in devices]
    return lax.ppermute(block, axis, route)


def silu_slope(pre_act):
    sigmoid_val = jax.nn.sigmoid(pre_act)
    return sigmoid_val * (1.0 + pre_act * (1.0 - sigmoid_val))


def in_groups(step_fn, running, shard_blocks, first_block):
    block_count = shard_blocks.shape[0]
    group_size = math.gcd(block_count, 32)
    if group_size == block_count:
        return step_fn(running, shard_blocks, first_block)

    def one_group(number, carried):
        segment = lax.dynamic_slice_in_dim(shard_blocks, number * group_size, group_size, 0)
        return step_fn(carried, segment, first_block + number * group_size)

    return lax.fori_loop(0, block_count // group_size, one_group, running)


def local(activations, out_grad, blocks, pattern, order):
    block_size = blocks.shape[-1]
    micro_count = activations.shape[1]
    tok_rows = activations.shape[1] * activations.shape[2]
    row_count = activations.shape[3] // block_size
    col_count = out_grad.shape[3] // block_size
    features = activations[0].reshape(tok_rows, row_count, block_size)
    hidden_grad = out_grad[0].reshape(tok_rows, out_grad.shape[3])
    own_blocks = blocks[0]
    all_indices = lax.all_gather(pattern[0], "fsdp", axis=0, tiled=True)

    def forward_step(running, shard_blocks, first_block):
        indices = lax.dynamic_slice_in_dim(all_indices, first_block, shard_blocks.shape[0], 0)
        rows_in = jnp.take(features, indices[:, 0], axis=1)
        product = jnp.einsum(
            "tbk,bkn->tbn", rows_in, shard_blocks, preferred_element_type=jnp.float32
        )
        return running.at[:, indices[:, 1]].add(product)

    pre_zero = jnp.zeros((tok_rows, col_count, block_size), jnp.float32)
    pre_act = in_groups(
        forward_step, pre_zero, lax.all_gather(own_blocks, "fsdp", axis=0, tiled=True), jnp.int32(0)
    )
    act_grad = (hidden_grad.astype(jnp.float32) * silu_slope(pre_act.reshape(tok_rows, -1))).astype(
        jnp.bfloat16
    )
    grad_cols = act_grad.reshape(tok_rows, col_count, block_size)

    def backward_step(running, shard_blocks, first_block):
        indices = lax.dynamic_slice_in_dim(all_indices, first_block, shard_blocks.shape[0], 0)
        cols_in = jnp.take(grad_cols, indices[:, 1], axis=1)
        product = jnp.einsum(
            "tbn,bkn->tbk", cols_in, shard_blocks, preferred_element_type=jnp.float32
        )
        return running.at[:, indices[:, 0]].add(product)

    back_zero = jnp.zeros((tok_rows, row_count, block_size), jnp.float32)
    input_grad = in_groups(
        backward_step,
        back_zero,
        lax.all_gather(own_blocks, "fsdp", axis=0, tiled=True),
        jnp.int32(0),
    )
    input_grad = input_grad.astype(jnp.bfloat16).reshape(
        micro_count, activations.shape[2], activations.shape[3]
    )
    ordered = jnp.take(input_grad, order, axis=0)
    received = passed_along(ordered, "section", -1)
    indices = all_indices
    rows_in = jnp.take(features, indices[:, 0], axis=1)
    cols_in = jnp.take(grad_cols, indices[:, 1], axis=1)
    owned_grads = lax.psum_scatter(
        jnp.einsum("tbk,tbn->bkn", rows_in, cols_in, preferred_element_type=jnp.float32),
        "fsdp",
        scatter_dimension=0,
        tiled=True,
    )
    summed = lax.psum(owned_grads, "dp")
    grad_scale = 1.0 / math.sqrt(tok_rows * lax.axis_size("fsdp") * lax.axis_size("dp"))
    return (received[None], (summed * grad_scale)[None])


def solution(mesh):
    in_specs = (
        P("section", None, ("fsdp", "dp"), None),
        P("section", None, ("fsdp", "dp"), None),
        P("section", "fsdp", None, None),
        P("section", "fsdp", None),
        P(),
    )
    out_specs = (P("section", None, ("fsdp", "dp"), None), P("section", "fsdp", None, None))
    return jax.shard_map(local, mesh=mesh, in_specs=in_specs, out_specs=out_specs, check_vma=False)
```

profile of v0, /device:TPU:0, one launch (start us, length us, event | category | flops | bytes accessed | tf_op | source)
XLA Modules:
  0.0 135.6 jit_solution(16365849403868641486)
XLA Ops:
  7.2 0.0 reduce-scatter.2.cloned.1.call-start
  7.2 0.8 copy.12
  8.0 13.6 %all-gather = s32[1,16,2]{2,0,1:T(1,128)S(1)} all-gather(s32[1,4,2]{2,0,1:T(1,128)S(1)} %copy.12), channel_id=2, replica_groups=mesh['section'=2,'fsdp'=4,'dp'=4] {'fsdp'}, dimensions={1}, use_global_device_ids=true | all-gather | bytes 160 | tf_op jit(solution)/shard_map/all_gather | solution.py:41
  21.6 0.1 copy.13
  21.7 1.6 %reshape_squeeze.4 = bf16[128,28,128]{2,1,0:T(8,128)(2,1)S(1)} reshape(bf16[1,4,32,3584]{3,2,1,0:T(8,128)(2,1)} %param.9) | data formatting | bytes 1835008 | tf_op jit(solution)/shard_map/reshape;squeeze | solution.py:38
  23.3 0.4 copy.14
  23.7 16.1 %all-gather.1 = bf16[1,16,128,128]{3,2,0,1:T(8,128)(2,1)S(1)} all-gather(bf16[1,4,128,128]{3,2,0,1:T(8,128)(2,1)} %bitcast.40), channel_id=3, replica_groups=mesh['section'=2,'fsdp'=4,'dp'=4] {'fsdp'}, dimensions={1}, use_global_device_ids=true | all-gather | bytes 655360 | tf_op jit(solution)/shard_map/all_gather | solution.py:72
  39.8 5.9 %copy.20 = f32[16,8,112,128]{3,2,1,0:T(8,128)} copy(bf16[16,8,112,128]{3,1,2,0:T(8,128)(2,1)} %bitcast.38) | data formatting | bytes 11010048
  45.7 0.6 gather_fusion.1
  46.3 0.4 fusion.6
  46.7 3.9 %broadcast_in_dim.46 = f32[128,112,128]{2,0,1:T(8,128)} broadcast(f32[]{:T(128)} %constant.23.clone.1), dimensions={} | broadcast | bytes 7340036 | tf_op jit(solution)/shard_map/broadcast_in_dim | solution.py:51
  50.6 3.4 %scatter_fusion = f32[128,112,128]{2,0,1:T(8,128)} fusion(f32[128,112,128]{2,0,1:T(8,128)} %broadcast_in_dim.46, s32[16]{0:T(128)S(1)} %get-tuple-element.10, f32[16,128,128]{2,1,0:T(8,128)S(1)} %fusion.6), kind=kCustom, calls=%fused_computation.3 | custom fusion | flops 262144 | bytes 3145792 | tf_op jit(solution)/shard_map/scatter-add | solution.py:49
  54.0 0.0 copy-start
  54.0 8.4 %fusion = bf16[128,112,128]{2,0,1:T(8,128)(2,1)} fusion(f32[128,112,128]{2,1,0:T(8,128)} %bitcast.37, f32[128,112,128]{2,0,1:T(8,128)} %scatter_fusion), kind=kLoop, calls=%fused_computation.6 | loop fusion | flops 16515072 | bytes 18350080 | tf_op jit(solution)/shard_map/convert_element_type | solution.py:55
  62.4 2.7 %gather_fusion.2 = bf16[16,128,128]{2,1,0:T(8,128)(2,1)S(1)} fusion(bf16[128,112,128]{2,0,1:T(8,128)(2,1)} %fusion, s32[1024]{0:T(1024)S(1)} %get-tuple-element.12), kind=kCustom, calls=%fused_computation.1.clone | custom fusion | bytes 1048640 | tf_op jit(solution)/shard_map/jit(_take)/gather | solution.py:62
  65.1 1.4 %fusion.1 = f32[16,128,128]{2,1,0:T(8,128)} fusion(bf16[16,128,128]{2,1,0:T(8,128)(2,1)S(1)} %gather_fusion.1, pred[16]{0:T(512)(128)(4,1)S(1)} %get-tuple-element.8, bf16[16,128,128]{2,1,0:T(8,128)(2,1)S(1)} %gather_fusion.2, pred[16]{0:T(512)(128)(4,1)S(1)} %get-tuple-element.4), kind=kOutput, calls=%fused_computation.8 | convolution fusion | flops 67633152 | bytes 2097184 | tf_op jit(solution)/shard_map/tbk,tbn->bkn/dot_general | solution.py:84
  66.5 0.0 reduce-scatter.2.cloned.1.call-update
  66.6 0.0 all-reduce.2.cloned.1.call-start
  66.6 0.5 fusion.3
  67.1 0.0 copy-done
  67.2 0.2 broadcast_in_dim.45
  67.4 1.6 %scatter_fusion.1 = f32[128,28,128]{2,0,1:T(8,128)S(1)} fusion(f32[128,28,128]{2,0,1:T(8,128)S(1)} %broadcast_in_dim.45, s32[16]{0:T(128)S(1)} %get-tuple-element.11, f32[16,128,128]{2,1,0:T(8,128)S(1)} %fusion.3), kind=kCustom, calls=%fused_computation.4 | custom fusion | flops 262144 | bytes 3145792 | tf_op jit(solution)/shard_map/scatter-add | solution.py:66
  69.0 0.1 convert_element_type.17
  69.1 0.6 copy.17
  69.8 0.5 reshape.27
  70.3 0.6 gather_fusion
  70.9 0.2 broadcast_select_fusion
  71.1 1.3 collective-permute-start
  72.4 20.7 %reduce-scatter.2.cloned.1.call-done = f32[4,128,128]{2,1,0:T(8,128)} async-done(((f32[16,128,128]{2,1,0:T(8,128)}), f32[4,128,128]{2,1,0:T(8,128)}) %reduce-scatter.2.cloned.1.call-update) | async-done | bytes 262160 | tf_op jit(solution)/shard_map/reduce_scatter | solution.py:83
  93.0 0.0 all-reduce.2.cloned.1.call-update
  93.1 0.0 collective-permute-done
  93.1 33.1 %all-reduce.2.cloned.1.call-done = f32[4,128,128]{2,1,0:T(8,128)} async-done(((f32[4,128,128]{2,1,0:T(8,128)}), f32[4,128,128]{2,1,0:T(8,128)}) %all-reduce.2.cloned.1.call-update) | async-done | bytes 262160 | tf_op jit(solution)/shard_map/psum | solution.py:89
  126.2 1.7 %multiply_bitcast_fusion = f32[1,4,128,128]{3,2,1,0:T(8,128)} fusion(f32[4,128,128]{2,1,0:T(8,128)} %all-reduce.2.cloned.1.call-done), kind=kLoop, calls=%fused_computation.19 | loop fusion | flops 65536 | bytes 524288 | tf_op jit(solution)/shard_map/broadcast_in_dim | solution.py:91
  127.9 0.9 copy.28
  (6 shorter events, 0.0 us)
Async XLA Ops:
  7.2 85.9 %reduce-scatter.2.cloned.1.call-start = ((), (), s32[]{:S(2)}) async-start(), calls=%async_computation.1 | async-start | bytes 1310720 | tf_op jit(solution)/shard_map/reduce_scatter | solution.py:83
  54.0 13.1 %copy-start = (s32[4]{0:T(128)S(1)}, s32[4]{0:T(128)}, u32[]{:S(2)}) copy-start(s32[4]{0:T(128)} %param.13) | copy-start | bytes 52
  66.6 59.6 %all-reduce.2.cloned.1.call-start = ((), (), s32[]{:S(2)}) async-start(), calls=%async_computation.2 | async-start | bytes 524288 | tf_op jit(solution)/shard_map/psum | solution.py:89
  71.1 22.0 %collective-permute-start = (bf16[4,32,3584]{2,1,0:T(8,128)(2,1)S(1)}, bf16[4,32,3584]{2,1,0:T(8,128)(2,1)S(1)}, u32[]{:S(2)}, u32[]{:S(2)}) collective-permute-start(bf16[4,32,3584]{2,1,0:T(8,128)(2,1)S(1)} %broadcast_select_fusion), channel_id=1, source_target_pairs={{16,0},{17,1},{18,2},{19,3},{20,4},{21,5},{22,6},{23,7},{24,8},{25... | collective-permute-start | bytes 2752520 | tf_op jit(solution)/shard_map/ppermute | solution.py:11
Sparse Core Ops, SparseCore 0:
  66.7 26.2 reduce-scatter.1
  95.4 30.7 all-reduce.1
where the time goes:
time: 136 us
  waiting for transfers between devices  53.8 us (40%)
  blocking collectives  29.7 us (22%)
  local copies, waits for them, and re-layouts  18.8 us (14%)
  other arithmetic  15.4 us (11%)
  between operations  14.2 us (10%)
  matrix products  2.29 us (2%)
  starting transfers between devices  1.37 us (1%)
    psum x1, waiting for transfers between devices, local(): summed = lax.psum(owned_grads, 'dp')  33.1 us
    reduce_scatter x1, waiting for transfers between devices, local(): lax.psum_scatter(jnp.einsum('tbk,tbn->bkn', rows_in, cols_in, preferred_e...  20.7 us
    all_gather x1, blocking collectives, local(): lax.all_gather(own_blocks, 'fsdp', axis=0, tiled=True)  16.1 us
    all_gather x1, blocking collectives, local(): all_indices = lax.all_gather(pattern[0], 'fsdp', axis=0, tiled=True)  13.6 us
    convert_element_type x1, other arithmetic, local(): (hidden_grad.astype(jnp.float32) * silu_slope(pre_act.reshape(tok_rows, -...  8.43 us
    unnamed x5, local copies, waits for them, and re-layouts  7.54 us
    broadcast_in_dim x1, local copies, waits for them, and re-layouts, local(): pre_zero = jnp.zeros((tok_rows, col_count, block_size), jnp.float32)  3.95 us
    scatter-add x1, other arithmetic, forward_step(): return running.at[:, indices[:, 1]].add(product)  3.38 us
  transfers between devices with their start and end apart: 3, of which 2 were waited for; matrix products, arithmetic and copies ran while one was open for 3% of the time, Pallas kernels for 0%

commit v1 on v0

--- a/solution.py
+++ b/solution.py
@@ -86,7 +86,7 @@
         scatter_dimension=0,
         tiled=True,
     )
-    summed = lax.psum(owned_grads, "dp")
+    summed = jnp.sum(lax.all_gather(owned_grads, "dp"), axis=0)
     grad_scale = 1.0 / math.sqrt(tok_rows * lax.axis_size("fsdp") * lax.axis_size("dp"))
     return (received[None], (summed * grad_scale)[None])
 

time: 136 us -> 127 us (0.934)
  waiting for transfers between devices: 53.8 us -> 44.5 us
    psum x1 -> x0, waiting for transfers between devices: 33.1 us -> none  [local(): summed = lax.psum(owned_grads, 'dp')]
    ppermute x1, waiting for transfers between devices: 0.01 us -> 22.3 us  [passed_along(): return lax.ppermute(block, axis, route)]
    broadcast_in_dim x1 -> x0, other arithmetic: 1.67 us -> none  [local(): return (received[None], (summed * grad_scale)[None])]
    reduce_scatter x1, waiting for transfers between devices: 20.7 us -> 22.1 us  [local(): lax.psum_scatter(jnp.einsum('tbk,tbn->bkn', rows_in, cols_in, preferred_e...]
where the time goes in v1:
time: 127 us
  waiting for transfers between devices  44.5 us (35%)
  blocking collectives  29.7 us (23%)
  local copies, waits for them, and re-layouts  18.8 us (15%)
  other arithmetic  15.8 us (12%)
  between operations  14.2 us (11%)
  matrix products  2.29 us (2%)
  starting transfers between devices  1.37 us (1%)
    ppermute x1, waiting for transfers between devices, passed_along(): return lax.ppermute(block, axis, route)  22.3 us
    reduce_scatter x1, waiting for transfers between devices, local(): lax.psum_scatter(jnp.einsum('tbk,tbn->bkn', rows_in, cols_in, preferred_e...  22.1 us
    all_gather x1, blocking collectives, local(): lax.all_gather(own_blocks, 'fsdp', axis=0, tiled=True)  16.1 us
    all_gather x1, blocking collectives, local(): all_indices = lax.all_gather(pattern[0], 'fsdp', axis=0, tiled=True)  13.6 us
    convert_element_type x1, other arithmetic, local(): (hidden_grad.astype(jnp.float32) * silu_slope(pre_act.reshape(tok_rows, -...  8.42 us
    unnamed x5, local copies, waits for them, and re-layouts  7.54 us
    broadcast_in_dim x1, local copies, waits for them, and re-layouts, local(): pre_zero = jnp.zeros((tok_rows, col_count, block_size), jnp.float32)  3.95 us
    scatter-add x1, other arithmetic, forward_step(): return running.at[:, indices[:, 1]].add(product)  3.38 us
  transfers between devices with their start and end apart: 3, of which 2 were waited for; matrix products, arithmetic and copies ran while one was open for 3% of the time, Pallas kernels for 0%

profile of v1, /device:TPU:0, one launch (start us, length us, event | category | flops | bytes accessed | tf_op | source)
XLA Modules:
  0.0 126.6 jit_solution(11105766843554003693)
XLA Ops:
  7.2 0.0 reduce-scatter.2.cloned.1.call-start
  7.2 0.8 copy.12
  8.0 13.6 %all-gather = s32[1,16,2]{2,0,1:T(1,128)S(1)} all-gather(s32[1,4,2]{2,0,1:T(1,128)S(1)} %copy.12), channel_id=2, replica_groups=mesh['section'=2,'fsdp'=4,'dp'=4] {'fsdp'}, dimensions={1}, use_global_device_ids=true | all-gather | bytes 160 | tf_op jit(solution)/shard_map/all_gather | solution.py:41
  21.6 0.1 copy.13
  21.7 1.6 %reshape_squeeze.4 = bf16[128,28,128]{2,1,0:T(8,128)(2,1)S(1)} reshape(bf16[1,4,32,3584]{3,2,1,0:T(8,128)(2,1)} %param.9) | data formatting | bytes 1835008 | tf_op jit(solution)/shard_map/reshape;squeeze | solution.py:38
  23.3 0.4 copy.14
  23.7 16.1 %all-gather.1 = bf16[1,16,128,128]{3,2,0,1:T(8,128)(2,1)S(1)} all-gather(bf16[1,4,128,128]{3,2,0,1:T(8,128)(2,1)} %bitcast.42), channel_id=3, replica_groups=mesh['section'=2,'fsdp'=4,'dp'=4] {'fsdp'}, dimensions={1}, use_global_device_ids=true | all-gather | bytes 655360 | tf_op jit(solution)/shard_map/all_gather | solution.py:72
  39.8 5.9 %copy.20 = f32[16,8,112,128]{3,2,1,0:T(8,128)} copy(bf16[16,8,112,128]{3,1,2,0:T(8,128)(2,1)} %bitcast.39) | data formatting | bytes 11010048
  45.7 0.6 gather_fusion.1
  46.3 0.4 fusion.6
  46.7 3.9 %broadcast_in_dim.44 = f32[128,112,128]{2,0,1:T(8,128)} broadcast(f32[]{:T(128)} %constant.10.clone.1), dimensions={} | broadcast | bytes 7340036 | tf_op jit(solution)/shard_map/broadcast_in_dim | solution.py:51
  50.6 3.4 %scatter_fusion = f32[128,112,128]{2,0,1:T(8,128)} fusion(f32[128,112,128]{2,0,1:T(8,128)} %broadcast_in_dim.44, s32[16]{0:T(128)S(1)} %get-tuple-element.10, f32[16,128,128]{2,1,0:T(8,128)S(1)} %fusion.6), kind=kCustom, calls=%fused_computation.3 | custom fusion | flops 262144 | bytes 3145792 | tf_op jit(solution)/shard_map/scatter-add | solution.py:49
  54.0 8.4 %fusion = bf16[128,112,128]{2,0,1:T(8,128)(2,1)} fusion(f32[128,112,128]{2,1,0:T(8,128)} %bitcast.38, f32[128,112,128]{2,0,1:T(8,128)} %scatter_fusion), kind=kLoop, calls=%fused_computation.6 | loop fusion | flops 16515072 | bytes 18350080 | tf_op jit(solution)/shard_map/convert_element_type | solution.py:55
  62.4 2.7 %gather_fusion.2 = bf16[16,128,128]{2,1,0:T(8,128)(2,1)S(1)} fusion(bf16[128,112,128]{2,0,1:T(8,128)(2,1)} %fusion, s32[1024]{0:T(1024)S(1)} %get-tuple-element.12), kind=kCustom, calls=%fused_computation.1.clone | custom fusion | bytes 1048640 | tf_op jit(solution)/shard_map/jit(_take)/gather | solution.py:62
  65.1 1.4 %fusion.1 = f32[16,128,128]{2,1,0:T(8,128)} fusion(bf16[16,128,128]{2,1,0:T(8,128)(2,1)S(1)} %gather_fusion.1, pred[16]{0:T(512)(128)(4,1)S(1)} %get-tuple-element.8, bf16[16,128,128]{2,1,0:T(8,128)(2,1)S(1)} %gather_fusion.2, pred[16]{0:T(512)(128)(4,1)S(1)} %get-tuple-element.4), kind=kOutput, calls=%fused_computation.8 | convolution fusion | flops 67633152 | bytes 2097184 | tf_op jit(solution)/shard_map/tbk,tbn->bkn/dot_general | solution.py:84
  66.5 0.0 copy-start
  66.5 0.0 reduce-scatter.2.cloned.1.call-update
  66.6 0.0 all-gather.5.cloned.1.call-start
  66.6 0.5 fusion.3
  67.1 0.2 broadcast_in_dim.43
  67.3 1.6 %scatter_fusion.1 = f32[128,28,128]{2,0,1:T(8,128)S(1)} fusion(f32[128,28,128]{2,0,1:T(8,128)S(1)} %broadcast_in_dim.43, s32[16]{0:T(128)S(1)} %get-tuple-element.11, f32[16,128,128]{2,1,0:T(8,128)S(1)} %fusion.3), kind=kCustom, calls=%fused_computation.4 | custom fusion | flops 262144 | bytes 3145792 | tf_op jit(solution)/shard_map/scatter-add | solution.py:66
  69.0 0.1 convert_element_type.17
  69.1 0.6 copy.17
  69.7 0.5 reshape.36
  70.2 0.0 copy-done
  70.3 0.6 gather_fusion
  70.9 22.1 %reduce-scatter.2.cloned.1.call-done = f32[4,128,128]{2,1,0:T(8,128)} async-done(((f32[16,128,128]{2,1,0:T(8,128)}), f32[4,128,128]{2,1,0:T(8,128)}) %reduce-scatter.2.cloned.1.call-update) | async-done | bytes 262160 | tf_op jit(solution)/shard_map/reduce_scatter | solution.py:83
  93.0 0.0 all-gather.5.cloned.1.call-update
  93.0 0.2 broadcast_select_fusion
  93.2 1.3 %collective-permute-start = (bf16[4,32,3584]{2,1,0:T(8,128)(2,1)S(1)}, bf16[4,32,3584]{2,1,0:T(8,128)(2,1)S(1)}, u32[]{:S(2)}, u32[]{:S(2)}) collective-permute-start(bf16[4,32,3584]{2,1,0:T(8,128)(2,1)S(1)} %broadcast_select_fusion), channel_id=1, source_target_pairs={{16,0},{17,1},{18,2},{19,3},{20,4},{21,5},{22,6},{23,7},{24,8},{25... | collective-permute-start | bytes 2752520 | tf_op jit(solution)/shard_map/ppermute | solution.py:11
  94.5 22.3 %collective-permute-done = bf16[4,32,3584]{2,1,0:T(8,128)(2,1)S(1)} collective-permute-done((bf16[4,32,3584]{2,1,0:T(8,128)(2,1)S(1)}, bf16[4,32,3584]{2,1,0:T(8,128)(2,1)S(1)}, u32[]{:S(2)}, u32[]{:S(2)}) %collective-permute-start) | collective-permute-done | bytes 917536 | tf_op jit(solution)/shard_map/ppermute | solution.py:11
  116.8 0.0 all-gather.5.cloned.1.call-done
  116.8 1.3 %reduce_sum.9 = f32[4,128,128]{2,1,0:T(8,128)S(1)} reduce(f32[4,4,128,128]{3,2,1,0:T(8,128)} %bitcast.40, f32[]{:T(128)} %constant.10.clone.1), dimensions={0}, to_apply=%region_3.6 | reduce | flops 196608 | bytes 1310724 | tf_op jit(solution)/shard_map/reduce_sum | solution.py:89
  118.1 0.7 multiply_bitcast_fusion
  118.8 0.9 copy.27
  (6 shorter events, 0.0 us)
Async XLA Ops:
  7.2 85.9 %reduce-scatter.2.cloned.1.call-start = ((), (), s32[]{:S(2)}) async-start(), calls=%async_computation.1 | async-start | bytes 1310720 | tf_op jit(solution)/shard_map/reduce_scatter | solution.py:83
  66.5 3.7 %copy-start = (s32[4]{0:T(128)S(1)}, s32[4]{0:T(128)}, u32[]{:S(2)}) copy-start(s32[4]{0:T(128)} %param.13) | copy-start | bytes 52
  66.6 50.2 %all-gather.5.cloned.1.call-start = ((), (), s32[]{:S(2)}) async-start(), calls=%async_computation.2 | async-start | bytes 1310720 | tf_op jit(solution)/shard_map/all_gather | solution.py:89
  93.2 23.6 %collective-permute-start = (bf16[4,32,3584]{2,1,0:T(8,128)(2,1)S(1)}, bf16[4,32,3584]{2,1,0:T(8,128)(2,1)S(1)}, u32[]{:S(2)}, u32[]{:S(2)}) collective-permute-start(bf16[4,32,3584]{2,1,0:T(8,128)(2,1)S(1)} %broadcast_select_fusion), channel_id=1, source_target_pairs={{16,0},{17,1},{18,2},{19,3},{20,4},{21,5},{22,6},{23,7},{24,8},{25... | collective-permute-start | bytes 2752520 | tf_op jit(solution)/shard_map/ppermute | solution.py:11
Sparse Core Ops, SparseCore 0:
  66.7 26.2 reduce-scatter.1
  94.6 15.1 all-gather.4
